TPU v7x, 512 devices: a whole 4x8x8 slice. The times are simulated.
512 devices in a mesh: dp: 32 (over y, x), section: 4 (over z_hi), space: 4 (over z_lo, core).
Axes of the slice: x: 4, y: 8, z: 8 (z_hi: 4, z_lo: 2; z = z_hi * 2 + z_lo), core: 2. Of those that a mesh axis runs over, the one named last changes fastest.
Arguments:
- images: bfloat16 [64, 4, 64, 256], P('dp', 'space'), may hold values from -6 to 6
- steps: int32 [64], P('dp'), may hold values from 0 to 999
- out_grad: bfloat16 [64, 4, 64, 256], P('dp', 'space'), may hold values from -0.125 to 0.125
- conv_weight: bfloat16 [4, 3, 3, 256, 256], P('section'), may hold values from -0.125 to 0.125
- gn_gain: float32 [4, 256], P('section'), may hold values from 0.5 to 2
- emb_weight: bfloat16 [4, 256, 512], P('section'), may hold values from -0.375 to 0.375
Outputs:
- grad_conv: float32 [4, 3, 3, 256, 256], P('section')
- grad_gain: float32 [4, 256], P('section')
- grad_emb: float32 [4, 256, 512], P('section')
All inputs are finite; a program needn't handle non-finite values.
Results may differ from a plain program's by a relative error of at most 0.0064.
Values may be sent and summed in bfloat16 or wider, within the bound.
No kernel may reach another device: no remote copies, remote signals or barrier semaphores. Data moves between devices by JAX's collectives and lax.ppermute only.
A program may use at most 64 MiB of HBM per device.

v0:
```python
import math
import jax
import jax.numpy as jnp
from jax import lax
from jax.sharding import Mesh, PartitionSpec as P

G = 32
FREQ = 256
MICRO = 2
EPS = 1e-05


def from_behind(value, axis, steps):
    count = lax.axis_size(axis)
    initial, last = (max(0, -steps), min(count, count - steps))
    return lax.ppermute(value, axis, [(source, source + steps) for source in range(initial, last)])


def extended(shard, sides, width):
    for axis, dim in sides:
        size, length = (lax.axis_size(axis), shard.shape[dim])
        up = [(i, (i + 1) % size) for i in range(size - 1)]
        down = [(j, i) for i, j in up]
        last = lax.slice_in_dim(shard, length - width, length, axis=dim)
        initial = lax.slice_in_dim(shard, 0, width, axis=dim)
        before = lax.ppermute(last, axis, up)
        after = lax.ppermute(initial, axis, down)
        shard = jnp.concatenate([before, shard, after], axis=dim)
    return shard


def sinusoid(timesteps, feature_n):
    half_n = feature_n // 2
    freqs = jnp.exp(-math.log(10000.0) * jnp.arange(half_n, dtype=jnp.float32) / half_n)
    angles = timesteps.astype(jnp.float32)[:, None] * freqs[None, :]
    return jnp.concatenate([jnp.cos(angles), jnp.sin(angles)], axis=1)


def group_sums(tensor, groups):
    batch_n, height_n, width_n, channels = tensor.shape
    split = tensor.reshape(batch_n, height_n, width_n, groups, channels // groups)
    return (jnp.sum(split, axis=(1, 2, 4)), jnp.sum(split * split, axis=(1, 2, 4)))


def spread(values, channels):
    return jnp.repeat(values, channels // values.shape[1], axis=1)[:, None, None, :]


def normalize(tensor, first_sum, square_sum, gains, scales, shifts, cell_count):
    channels = tensor.shape[3]
    average = first_sum / cell_count
    inverse = lax.rsqrt(square_sum / cell_count - average * average + EPS)
    normed = (tensor - spread(average, channels)) * spread(inverse, channels) * gains
    return normed * (1.0 + scales[:, None, None, :]) + shifts[:, None, None, :]


def patches(padded, height_n, width_n):
    return jnp.concatenate(
        [
            padded[:, vertical : vertical + height_n, lateral : lateral + width_n, :]
            for vertical in range(3)
            for lateral in range(3)
        ],
        axis=3,
    )


def convolve(padded, matrix):
    batch_n, height_p, width_p, channels = padded.shape
    flat = patches(padded, height_p - 2, width_p - 2).reshape(-1, 9 * channels)
    return jnp.dot(flat, matrix, preferred_element_type=jnp.float32).reshape(
        batch_n, height_p - 2, width_p - 2, matrix.shape[1]
    )


def flip_weight(weight):
    channels = weight.shape[2]
    return jnp.transpose(weight[::-1, ::-1], (0, 1, 3, 2)).reshape(9 * channels, channels)


def silu_slope(pre_act):
    sigmoid_v = jax.nn.sigmoid(pre_act)
    return sigmoid_v * (1.0 + pre_act * (1.0 - sigmoid_v))


def pad_columns(tensor):
    return jnp.pad(tensor, ((0, 0), (0, 0), (1, 1), (0, 0)))


def pick(stacked, index):
    return lax.dynamic_index_in_dim(stacked, index, 0, keepdims=False)


def norm_backward(tensor, first_sum, square_sum, gains, scales, shifts, cell_count, d_pre):

    def mapping(tensor_v, first_v, square_v, gains_v, scales_v, shifts_v):
        return normalize(tensor_v, first_v, square_v, gains_v, scales_v, shifts_v, cell_count)

    _, pull_back = jax.vjp(mapping, tensor, first_sum, square_sum, gains, scales, shifts)
    return pull_back(d_pre)


def pad_both(tensor):
    return jnp.pad(tensor, ((0, 0), (1, 1), (1, 1), (0, 0)))


def group_blocks(channels):
    group = jnp.arange(channels) // (channels // G)
    return (group[:, None] == group[None, :]).astype(jnp.float32)


def over_groups(values, blocks):
    return jnp.dot(values, blocks, precision=lax.Precision.HIGHEST)


def normalize_spread(tensor, first_c, square_c, gains, scales, shifts, cell_count):
    average = first_c / cell_count
    inverse = lax.rsqrt(square_c / cell_count - average * average + EPS)
    normed = (tensor - average[:, None, None, :]) * inverse[:, None, None, :] * gains
    return normed * (1.0 + scales[:, None, None, :]) + shifts[:, None, None, :]


def conv_same(tensor, kernel):
    return lax.conv_general_dilated(
        tensor,
        kernel,
        (1, 1),
        ((1, 1), (1, 1)),
        dimension_numbers=("NHWC", "HWIO", "NHWC"),
        preferred_element_type=jnp.float32,
    )


def block_forward(inputs, flat_weight, gains, scales, shifts, cell_count):
    tensor = inputs.astype(jnp.float32)
    blocks = group_blocks(tensor.shape[3])
    first_c = over_groups(jnp.sum(tensor, axis=(1, 2)), blocks)
    square_c = over_groups(jnp.sum(tensor * tensor, axis=(1, 2)), blocks)
    pre_act = normalize_spread(tensor, first_c, square_c, gains, scales, shifts, cell_count)
    activation = jax.nn.silu(pre_act).astype(jnp.bfloat16)
    padded = pad_both(activation)
    output = (tensor + conv_same(activation, flat_weight)).astype(jnp.bfloat16)
    return (output, (first_c, square_c, padded))


def block_backward(upstream, inputs, saved, flipped, gains, scales, shifts, cell_count):
    first_c, square_c, _ = saved
    tensor = inputs.astype(jnp.float32)
    blocks = group_blocks(tensor.shape[3])
    pre_act = normalize_spread(tensor, first_c, square_c, gains, scales, shifts, cell_count)
    d_act = conv_same(upstream, flipped)
    d_pre = d_act * silu_slope(pre_act)

    def mapping(tensor_v, first_v, square_v, gains_v, scales_v, shifts_v):
        return normalize_spread(
            tensor_v, first_v, square_v, gains_v, scales_v, shifts_v, cell_count
        )

    _, pull_back = jax.vjp(mapping, tensor, first_c, square_c, gains, scales, shifts)
    d_tensor, d_first, d_square, d_gains, d_scales, d_shifts = pull_back(d_pre)
    d_first = over_groups(d_first, blocks)[:, None, None, :]
    d_square = over_groups(d_square, blocks)[:, None, None, :]
    d_tensor = d_tensor + d_first + 2.0 * tensor * d_square
    d_input = (upstream.astype(jnp.float32) + d_tensor).astype(jnp.bfloat16)
    return (d_input, (d_gains, d_scales, d_shifts))


def keep(flag, new, old):
    return jax.tree.map(lambda a, b: jnp.where(flag, a, b), new, old)


def per_device(images, steps, out_grad, conv_weight, gn_gain, emb_weight):
    section_count = lax.axis_size("section")
    section_no = lax.axis_index("section")
    images = lax.all_gather(images, "space", axis=1, tiled=True)
    out_grad = lax.all_gather(out_grad, "space", axis=1, tiled=True)
    row_count = images.shape[1]
    col_count = images.shape[2]
    channels = images.shape[3]
    cell_count = row_count * col_count * (channels // G)
    weight = conv_weight[0]
    flat_weight = weight
    flipped = jnp.transpose(weight[::-1, ::-1], (0, 1, 3, 2))
    gains = gn_gain[0]
    features = sinusoid(steps, FREQ)
    embedded = jnp.dot(features, emb_weight[0].astype(jnp.float32), precision=lax.Precision.HIGHEST)
    scales = embedded[:, :channels]
    shifts = embedded[:, channels:]
    last = section_count - 1
    carried = images
    kept = None
    for moment in range(section_count):
        inputs = images
        if moment > 0:
            inputs = lax.ppermute(carried, "section", [(moment - 1, moment)])
        if moment == last:
            inputs = (inputs.astype(jnp.float32) + skip.astype(jnp.float32)).astype(jnp.bfloat16)
        output, saved = block_forward(inputs, flat_weight, gains, scales, shifts, cell_count)
        if moment == 0:
            skip = lax.ppermute(output, "section", [(0, last)])
        state = (inputs, saved)
        kept = state if kept is None else keep(section_no == moment, state, kept)
        carried = output
    kept_in, kept_saved = kept
    carried = out_grad
    kept = None
    for moment in range(section_count):
        active = last - moment
        upstream = out_grad
        if moment > 0:
            upstream = lax.ppermute(carried, "section", [(active + 1, active)])
        if active == 0:
            upstream = (upstream.astype(jnp.float32) + skip_grad.astype(jnp.float32)).astype(
                jnp.bfloat16
            )
        d_input, pieces = block_backward(
            upstream, kept_in, kept_saved, flipped, gains, scales, shifts, cell_count
        )
        if moment == 0:
            skip_grad = lax.ppermute(d_input, "section", [(last, 0)])
        state = (upstream, pieces)
        kept = state if kept is None else keep(section_no == active, state, kept)
        carried = d_input
    kept_up, (d_gains, d_scales, d_shifts) = kept
    space_count = lax.axis_size("space")
    space_no = quarter_of(lax.axis_index("space"), space_count)
    patch_rows = 9 * channels // space_count
    flat_patch = patches(kept_saved[2], row_count, col_count).reshape(-1, 9 * channels)
    own_patch = lax.dynamic_slice_in_dim(flat_patch, space_no * patch_rows, patch_rows, axis=1)
    weight_grad = jnp.dot(
        own_patch.T, kept_up.reshape(-1, channels), preferred_element_type=jnp.float32
    )
    emb_rows = FREQ // space_count
    own_features = lax.dynamic_slice_in_dim(features, space_no * emb_rows, emb_rows, axis=1)
    emb_grad = jnp.dot(
        own_features.T,
        jnp.concatenate([d_scales, d_shifts], axis=1),
        precision=lax.Precision.HIGHEST,
    )
    return reduce_grads(weight_grad, d_gains, emb_grad)


def butterfly_scatter(flat, axis):
    count = lax.axis_size(axis)
    index = lax.axis_index(axis)
    step = 1
    while step < count:
        bit = index // step % 2
        half = flat.shape[0] // 2
        kept = lax.dynamic_slice_in_dim(flat, bit * half, half, 0)
        sent = lax.dynamic_slice_in_dim(flat, (1 - bit) * half, half, 0)
        flat = kept + lax.ppermute(sent, axis, [(j, j ^ step) for j in range(count)])
        step *= 2
    return flat


def butterfly_sum(flat, axis):
    count = lax.axis_size(axis)
    step = 1
    while step < count:
        flat = flat + lax.ppermute(flat, axis, [(j, j ^ step) for j in range(count)])
        step *= 2
    return flat


def butterfly_gather(flat, axis, steps):
    count = lax.axis_size(axis)
    index = lax.axis_index(axis)
    for step in steps:
        bit = index // step % 2
        got = lax.ppermute(flat, axis, [(j, j ^ step) for j in range(count)])
        length = flat.shape[0]
        joined = jnp.concatenate([flat, flat])
        flat = lax.dynamic_update_slice_in_dim(joined, got, (1 - bit) * length, 0)
    return flat


def descending(count):
    steps = []
    step = count // 2
    while step >= 1:
        steps.append(step)
        step //= 2
    return steps


def quarter_of(space_no, space_count):
    return space_no % 2 * (space_count // 2) + space_no // 2


def reduce_grads(weight_grad, gain_grad, emb_grad):
    channels = gain_grad.shape[0]
    parts = [weight_grad, emb_grad.reshape(-1, channels), gain_grad[None]]
    rows = sum((part.shape[0] for part in parts))
    devices = lax.axis_size("dx")
    padded_rows = -(-rows // (8 * devices)) * 8 * devices
    parts.append(jnp.zeros((padded_rows - rows, channels), jnp.float32))
    flat = jnp.concatenate(parts, axis=0)
    flat = butterfly_scatter(flat, "dx")
    flat = butterfly_sum(flat, "dy")
    flat = butterfly_gather(flat.astype(jnp.bfloat16), "dx", descending(lax.axis_size("dx")))
    space_count = lax.axis_size("space")
    flat = butterfly_gather(flat, "space", descending(space_count))
    flat = flat.reshape(space_count, padded_rows, channels).astype(jnp.float32)
    weight_rows = weight_grad.shape[0]
    emb_rows = emb_grad.size // channels
    conv = flat[:, :weight_rows].reshape(1, 3, 3, channels, channels)
    emb = flat[:, weight_rows : weight_rows + emb_rows].reshape(
        1, emb_grad.shape[0] * space_count, -1
    )
    gain = flat[0, weight_rows + emb_rows][None]
    return (conv, gain, emb)


def solution(mesh):
    dp_n = mesh.shape["dp"]
    dx_n = 4 if dp_n % 4 == 0 else 1
    mesh = Mesh(
        mesh.devices.reshape(dp_n // dx_n, dx_n, *mesh.devices.shape[1:]),
        ("dy", "dx", "section", "space"),
    )
    data = ("dy", "dx")
    in_specs = (
        P(data, "space", None, None),
        P(data),
        P(data, "space", None, None),
        P("section", None, None, None, None),
        P("section", None),
        P("section", None, None),
    )
    out_specs = (P("section", None, None, None, None), P("section", None), P("section", None, None))
    return jax.shard_map(
        per_device, mesh=mesh, in_specs=in_specs, out_specs=out_specs, check_vma=False
    )
```

profile of v0, /device:TPU:25, one launch (start us, length us, event | category | flops | bytes accessed | tf_op | source)
XLA Modules:
  0.0 192.3 jit_solution(9327620106959557601)
XLA Ops:
  0.7 7.5 %all_gather.6 = bf16[2,4,64,256]{3,2,0,1:T(8,128)(2,1)S(1)} all-gather(bf16[2,1,64,256]{3,2,0,1:T(8,128)(2,1)} %bitcast.164), channel_id=1, replica_groups=mesh['dy'=8,'dx'=4,'section'=4,'space'=4] {'space'}, dimensions={1}, use_global_device_ids=true | all-gather | bytes 327680 | tf_op jit(solution)/shard_map/all_gather | solution.py:175
  8.4 0.7 convert_element_type.101
  9.2 1.2 fusion.130
  10.9 1.2 fusion.221
  13.0 0.9 convolution_select_fusion.6
  14.5 5.8 %collective-permute-start = (bf16[2,4,64,256]{3,1,2,0:T(4,128)(2,1)S(1)}, bf16[2,4,64,256]{3,1,2,0:T(4,128)(2,1)S(1)}, u32[]{:S(2)}, u32[]{:S(2)}) collective-permute-start(bf16[2,4,64,256]{3,1,2,0:T(4,128)(2,1)S(1)} %fusion.79), channel_id=1, source_target_pairs={{0,4},{1,5},{2,6},{3,7},{16,20},{17,21},{18,22},{19,23},{32,36},{3... | collective-permute-start | bytes 786440 | tf_op jit(solution)/shard_map/ppermute | solution.py:195
  20.3 4.7 %collective-permute-start.3 = (bf16[2,4,64,256]{3,1,2,0:T(4,128)(2,1)S(1)}, bf16[2,4,64,256]{3,1,2,0:T(4,128)(2,1)S(1)}, u32[]{:S(2)}, u32[]{:S(2)}) collective-permute-start(bf16[2,4,64,256]{3,1,2,0:T(4,128)(2,1)S(1)} %fusion.79), channel_id=1, source_target_pairs={{0,12},{1,13},{2,14},{3,15},{16,28},{17,29},{18,30},{19,31},{32,44... | collective-permute-start | bytes 786440 | tf_op jit(solution)/shard_map/ppermute | solution.py:200
  25.1 10.5 %all_gather.7 = bf16[2,4,64,256]{3,2,0,1:T(8,128)(2,1)S(1)} all-gather(bf16[2,1,64,256]{3,2,0,1:T(8,128)(2,1)S(1)} %bitcast.165), channel_id=1, replica_groups=mesh['dy'=8,'dx'=4,'section'=4,'space'=4] {'space'}, dimensions={1}, use_global_device_ids=true | all-gather | bytes 327680 | tf_op jit(solution)/shard_map/all_gather | solution.py:176
  36.5 0.9 convolution_select_fusion.3
  40.4 0.9 convolution_select_fusion.5
  41.8 0.9 collective-permute-start.1
  45.2 0.8 convolution_select_fusion.4
  46.6 0.7 collective-permute-start.2
  48.6 1.8 multiply_reduce_fusion
  51.3 0.7 collective-permute-start.4
  52.0 1.3 collective-permute-start.7
  53.3 0.7 select_select_fusion
  55.7 0.9 convolution_select_fusion.2
  56.9 0.7 multiply_reduce_fusion.1
  58.6 0.9 collective-permute-start.5
  60.7 0.9 convolution_select_fusion.1
  62.0 0.7 multiply_reduce_fusion.2
  63.7 1.3 collective-permute-start.6
  65.3 1.6 copy.82
  67.0 2.4 %collective-permute-done.7 = bf16[2,4,64,256]{3,1,2,0:T(4,128)(2,1)S(1)} collective-permute-done((bf16[2,4,64,256]{3,1,2,0:T(4,128)(2,1)S(1)}, bf16[2,4,64,256]{3,1,2,0:T(4,128)(2,1)S(1)}, u32[]{:S(2)}, u32[]{:S(2)}) %collective-permute-start.7) | collective-permute-done | bytes 262176 | tf_op jit(solution)/shard_map/ppermute | solution.py:220
  69.4 19.1 %collective-permute-done.6 = bf16[2,4,64,256]{3,1,2,0:T(4,128)(2,1)S(1)} collective-permute-done((bf16[2,4,64,256]{3,1,2,0:T(4,128)(2,1)S(1)}, bf16[2,4,64,256]{3,1,2,0:T(4,128)(2,1)S(1)}, u32[]{:S(2)}, u32[]{:S(2)}) %collective-permute-start.6) | collective-permute-done | bytes 262176 | tf_op jit(solution)/shard_map/ppermute | solution.py:211
  90.0 0.9 convolution_select_fusion
  92.2 1.8 fusion.55
  94.3 3.1 %collective-permute-start.8 = (f32[368,256]{1,0:T(8,128)S(1)}, f32[368,256]{1,0:T(8,128)S(1)}, u32[]{:S(2)}, u32[]{:S(2)}) collective-permute-start(f32[368,256]{1,0:T(8,128)S(1)} %constant_dynamic-slice_fusion.2), channel_id=1, source_target_pairs={{0,16},{16,0},{32,48},{48,32},{1,17},{17,1},{33,49},{49,33},{2,18}... | collective-permute-start | bytes 1130504 | tf_op jit(solution)/shard_map/ppermute | solution.py:252
  97.4 5.2 %collective-permute-done.8 = f32[368,256]{1,0:T(8,128)S(1)} collective-permute-done((f32[368,256]{1,0:T(8,128)S(1)}, f32[368,256]{1,0:T(8,128)S(1)}, u32[]{:S(2)}, u32[]{:S(2)}) %collective-permute-start.8) | collective-permute-done | bytes 376864 | tf_op jit(solution)/shard_map/ppermute | solution.py:252
  102.7 4.7 %collective-permute-start.9 = (f32[184,256]{1,0:T(8,128)S(1)}, f32[184,256]{1,0:T(8,128)S(1)}, u32[]{:S(2)}, u32[]{:S(2)}) collective-permute-start(f32[184,256]{1,0:T(8,128)S(1)} %constant_dynamic-slice_fusion.1), channel_id=1, source_target_pairs={{0,32},{16,48},{32,0},{48,16},{1,33},{17,49},{33,1},{49,17},{2,34}... | collective-permute-start | bytes 565256 | tf_op jit(solution)/shard_map/ppermute | solution.py:252
  107.4 3.9 %collective-permute-done.9 = f32[184,256]{1,0:T(8,128)S(1)} collective-permute-done((f32[184,256]{1,0:T(8,128)S(1)}, f32[184,256]{1,0:T(8,128)S(1)}, u32[]{:S(2)}, u32[]{:S(2)}) %collective-permute-start.9) | collective-permute-done | bytes 188448 | tf_op jit(solution)/shard_map/ppermute | solution.py:252
  111.3 2.1 %collective-permute-start.10 = (f32[184,256]{1,0:T(8,128)S(1)}, f32[184,256]{1,0:T(8,128)S(1)}, u32[]{:S(2)}, u32[]{:S(2)}) collective-permute-start(f32[184,256]{1,0:T(8,128)S(1)} %dynamic-slice_add_fusion.1), channel_id=1, source_target_pairs={{0,64},{64,0},{128,192},{192,128},{256,320},{320,256},{384,448},{4... | collective-permute-start | bytes 565256 | tf_op jit(solution)/shard_map/ppermute | solution.py:261
  113.3 4.3 %collective-permute-done.10 = f32[184,256]{1,0:T(8,128)S(1)} collective-permute-done((f32[184,256]{1,0:T(8,128)S(1)}, f32[184,256]{1,0:T(8,128)S(1)}, u32[]{:S(2)}, u32[]{:S(2)}) %collective-permute-start.10) | collective-permute-done | bytes 188448 | tf_op jit(solution)/shard_map/ppermute | solution.py:261
  117.6 2.0 %collective-permute-start.11 = (f32[184,256]{1,0:T(8,128)S(1)}, f32[184,256]{1,0:T(8,128)S(1)}, u32[]{:S(2)}, u32[]{:S(2)}) collective-permute-start(f32[184,256]{1,0:T(8,128)S(1)} %add.291), channel_id=1, source_target_pairs={{0,128},{64,192},{128,0},{192,64},{256,384},{320,448},{384,256},{4... | collective-permute-start | bytes 565256 | tf_op jit(solution)/shard_map/ppermute | solution.py:261
  119.6 7.2 %collective-permute-done.11 = f32[184,256]{1,0:T(8,128)S(1)} collective-permute-done((f32[184,256]{1,0:T(8,128)S(1)}, f32[184,256]{1,0:T(8,128)S(1)}, u32[]{:S(2)}, u32[]{:S(2)}) %collective-permute-start.11) | collective-permute-done | bytes 188448 | tf_op jit(solution)/shard_map/ppermute | solution.py:261
  126.9 4.0 %collective-permute-start.12 = (f32[184,256]{1,0:T(8,128)S(1)}, f32[184,256]{1,0:T(8,128)S(1)}, u32[]{:S(2)}, u32[]{:S(2)}) collective-permute-start(f32[184,256]{1,0:T(8,128)S(1)} %add.292), channel_id=1, source_target_pairs={{0,256},{64,320},{128,384},{192,448},{256,0},{320,64},{384,128},{4... | collective-permute-start | bytes 565256 | tf_op jit(solution)/shard_map/ppermute | solution.py:261
  130.9 7.6 %collective-permute-done.12 = f32[184,256]{1,0:T(8,128)S(1)} collective-permute-done((f32[184,256]{1,0:T(8,128)S(1)}, f32[184,256]{1,0:T(8,128)S(1)}, u32[]{:S(2)}, u32[]{:S(2)}) %collective-permute-start.12) | collective-permute-done | bytes 188448 | tf_op jit(solution)/shard_map/ppermute | solution.py:261
  138.5 6.4 %collective-permute-start.13 = (bf16[184,256]{1,0:T(8,128)(2,1)S(1)}, bf16[184,256]{1,0:T(8,128)(2,1)S(1)}, u32[]{:S(2)}, u32[]{:S(2)}) collective-permute-start(bf16[184,256]{1,0:T(8,128)(2,1)S(1)} %add_convert_fusion.2), channel_id=1, source_target_pairs={{0,32},{16,48},{32,0},{48,16},{1,33},{17,49},{33,1},{49,17},{2,34}... | collective-permute-start | bytes 282632 | tf_op jit(solution)/shard_map/ppermute | solution.py:271
  145.0 1.9 %collective-permute-done.13 = bf16[184,256]{1,0:T(8,128)(2,1)S(1)} collective-permute-done((bf16[184,256]{1,0:T(8,128)(2,1)S(1)}, bf16[184,256]{1,0:T(8,128)(2,1)S(1)}, u32[]{:S(2)}, u32[]{:S(2)}) %collective-permute-start.13) | collective-permute-done | bytes 94240 | tf_op jit(solution)/shard_map/ppermute | solution.py:271
  146.9 3.3 %collective-permute-start.14 = (bf16[368,256]{1,0:T(8,128)(2,1)S(1)}, bf16[368,256]{1,0:T(8,128)(2,1)S(1)}, u32[]{:S(2)}, u32[]{:S(2)}) collective-permute-start(bf16[368,256]{1,0:T(8,128)(2,1)S(1)} %constant_dynamic-update-slice_fusion.3), channel_id=1, source_target_pairs={{0,16},{16,0},{32,48},{48,32},{1,17},{17,1},{33,49},{49,33},{2,18}... | collective-permute-start | bytes 565256 | tf_op jit(solution)/shard_map/ppermute | solution.py:271
  150.3 2.9 %collective-permute-done.14 = bf16[368,256]{1,0:T(8,128)(2,1)S(1)} collective-permute-done((bf16[368,256]{1,0:T(8,128)(2,1)S(1)}, bf16[368,256]{1,0:T(8,128)(2,1)S(1)}, u32[]{:S(2)}, u32[]{:S(2)}) %collective-permute-start.14) | collective-permute-done | bytes 188448 | tf_op jit(solution)/shard_map/ppermute | solution.py:271
  153.2 10.6 %collective-permute-start.15 = (bf16[736,256]{1,0:T(8,128)(2,1)S(1)}, bf16[736,256]{1,0:T(8,128)(2,1)S(1)}, u32[]{:S(2)}, u32[]{:S(2)}) collective-permute-start(bf16[736,256]{1,0:T(8,128)(2,1)S(1)} %constant_dynamic-update-slice_fusion.2), channel_id=1, source_target_pairs={{0,2},{1,3},{2,0},{3,1},{4,6},{5,7},{6,4},{7,5},{8,10},{9,11},{10,... | collective-permute-start | bytes 1130504 | tf_op jit(solution)/shard_map/ppermute | solution.py:271
  163.9 4.9 %collective-permute-done.15 = bf16[736,256]{1,0:T(8,128)(2,1)S(1)} collective-permute-done((bf16[736,256]{1,0:T(8,128)(2,1)S(1)}, bf16[736,256]{1,0:T(8,128)(2,1)S(1)}, u32[]{:S(2)}, u32[]{:S(2)}) %collective-permute-start.15) | collective-permute-done | bytes 376864 | tf_op jit(solution)/shard_map/ppermute | solution.py:271
  168.9 18.2 %collective-permute-start.16 = (bf16[1472,256]{1,0:T(8,128)(2,1)S(1)}, bf16[1472,256]{1,0:T(8,128)(2,1)S(1)}, u32[]{:S(2)}, u32[]{:S(2)}) collective-permute-start(bf16[1472,256]{1,0:T(8,128)(2,1)S(1)} %constant_dynamic-update-slice_fusion.1), channel_id=1, source_target_pairs={{0,1},{1,0},{2,3},{3,2},{4,5},{5,4},{6,7},{7,6},{8,9},{9,8},{10,11... | collective-permute-start | bytes 2261000 | tf_op jit(solution)/shard_map/ppermute | solution.py:271
  187.2 1.7 collective-permute-done.16
  189.2 1.6 slice.95
  191.4 0.9 reshape.165
  (121 shorter events, 21.9 us)
Async XLA Ops:
  0.6 12.3 %copy-start = (bf16[1,3,3,256,256]{4,3,2,1,0:T(8,128)(2,1)S(1)}, bf16[1,3,3,256,256]{4,3,2,1,0:T(8,128)(2,1)}, u32[]{:S(2)}) copy-start(bf16[1,3,3,256,256]{4,3,2,1,0:T(8,128)(2,1)} %param.9) | copy-start | bytes 3538948
  0.6 12.3 %copy-start.3 = (pred[16,9]{0,1:T(8,128)(4,1)S(1)}, pred[16,9]{0,1:T(8,128)(4,1)}, u32[]{:S(2)}) copy-start(pred[16,9]{0,1:T(8,128)(4,1)} %constant.217) | copy-start | bytes 436
  13.0 12.1 %copy-start.2 = (bf16[2,1,64,256]{3,2,1,0:T(8,128)(2,1)S(1)}, bf16[2,1,64,256]{3,2,1,0:T(8,128)(2,1)}, u32[]{:S(2)}) copy-start(bf16[2,1,64,256]{3,2,1,0:T(8,128)(2,1)} %param.8) | copy-start | bytes 196612
  14.5 23.8 %collective-permute-start = (bf16[2,4,64,256]{3,1,2,0:T(4,128)(2,1)S(1)}, bf16[2,4,64,256]{3,1,2,0:T(4,128)(2,1)S(1)}, u32[]{:S(2)}, u32[]{:S(2)}) collective-permute-start(bf16[2,4,64,256]{3,1,2,0:T(4,128)(2,1)S(1)} %fusion.79), channel_id=1, source_target_pairs={{0,4},{1,5},{2,6},{3,7},{16,20},{17,21},{18,22},{19,23},{32,36},{3... | collective-permute-start | bytes 786440 | tf_op jit(solution)/shard_map/ppermute | solution.py:195
  20.3 27.4 %collective-permute-start.3 = (bf16[2,4,64,256]{3,1,2,0:T(4,128)(2,1)S(1)}, bf16[2,4,64,256]{3,1,2,0:T(4,128)(2,1)S(1)}, u32[]{:S(2)}, u32[]{:S(2)}) collective-permute-start(bf16[2,4,64,256]{3,1,2,0:T(4,128)(2,1)S(1)} %fusion.79), channel_id=1, source_target_pairs={{0,12},{1,13},{2,14},{3,15},{16,28},{17,29},{18,30},{19,31},{32,44... | collective-permute-start | bytes 786440 | tf_op jit(solution)/shard_map/ppermute | solution.py:200
  36.1 1.8 copy-start.1
  41.8 1.3 collective-permute-start.1
  46.6 1.1 collective-permute-start.2
  51.3 3.4 %collective-permute-start.4 = (bf16[2,4,64,256]{3,1,2,0:T(4,128)(2,1)S(1)}, bf16[2,4,64,256]{3,1,2,0:T(4,128)(2,1)S(1)}, u32[]{:S(2)}, u32[]{:S(2)}) collective-permute-start(bf16[2,4,64,256]{3,1,2,0:T(4,128)(2,1)S(1)} %fusion.94), channel_id=1, source_target_pairs={{12,8},{13,9},{14,10},{15,11},{28,24},{29,25},{30,26},{31,27},{44,... | collective-permute-start | bytes 786440 | tf_op jit(solution)/shard_map/ppermute | solution.py:211
  52.0 17.4 %collective-permute-start.7 = (bf16[2,4,64,256]{3,1,2,0:T(4,128)(2,1)S(1)}, bf16[2,4,64,256]{3,1,2,0:T(4,128)(2,1)S(1)}, u32[]{:S(2)}, u32[]{:S(2)}) collective-permute-start(bf16[2,4,64,256]{3,1,2,0:T(4,128)(2,1)S(1)} %fusion.94), channel_id=1, source_target_pairs={{12,0},{13,1},{14,2},{15,3},{28,16},{29,17},{30,18},{31,19},{44,32... | collective-permute-start | bytes 786440 | tf_op jit(solution)/shard_map/ppermute | solution.py:220
  58.6 1.3 collective-permute-start.5
  63.7 24.8 %collective-permute-start.6 = (bf16[2,4,64,256]{3,1,2,0:T(4,128)(2,1)S(1)}, bf16[2,4,64,256]{3,1,2,0:T(4,128)(2,1)S(1)}, u32[]{:S(2)}, u32[]{:S(2)}) collective-permute-start(bf16[2,4,64,256]{3,1,2,0:T(4,128)(2,1)S(1)} %fusion.100), channel_id=1, source_target_pairs={{4,0},{5,1},{6,2},{7,3},{20,16},{21,17},{22,18},{23,19},{36,32},{3... | collective-permute-start | bytes 786440 | tf_op jit(solution)/shard_map/ppermute | solution.py:211
  94.3 8.3 %collective-permute-start.8 = (f32[368,256]{1,0:T(8,128)S(1)}, f32[368,256]{1,0:T(8,128)S(1)}, u32[]{:S(2)}, u32[]{:S(2)}) collective-permute-start(f32[368,256]{1,0:T(8,128)S(1)} %constant_dynamic-slice_fusion.2), channel_id=1, source_target_pairs={{0,16},{16,0},{32,48},{48,32},{1,17},{17,1},{33,49},{49,33},{2,18}... | collective-permute-start | bytes 1130504 | tf_op jit(solution)/shard_map/ppermute | solution.py:252
  102.7 8.5 %collective-permute-start.9 = (f32[184,256]{1,0:T(8,128)S(1)}, f32[184,256]{1,0:T(8,128)S(1)}, u32[]{:S(2)}, u32[]{:S(2)}) collective-permute-start(f32[184,256]{1,0:T(8,128)S(1)} %constant_dynamic-slice_fusion.1), channel_id=1, source_target_pairs={{0,32},{16,48},{32,0},{48,16},{1,33},{17,49},{33,1},{49,17},{2,34}... | collective-permute-start | bytes 565256 | tf_op jit(solution)/shard_map/ppermute | solution.py:252
  111.3 6.3 %collective-permute-start.10 = (f32[184,256]{1,0:T(8,128)S(1)}, f32[184,256]{1,0:T(8,128)S(1)}, u32[]{:S(2)}, u32[]{:S(2)}) collective-permute-start(f32[184,256]{1,0:T(8,128)S(1)} %dynamic-slice_add_fusion.1), channel_id=1, source_target_pairs={{0,64},{64,0},{128,192},{192,128},{256,320},{320,256},{384,448},{4... | collective-permute-start | bytes 565256 | tf_op jit(solution)/shard_map/ppermute | solution.py:261
  117.6 9.2 %collective-permute-start.11 = (f32[184,256]{1,0:T(8,128)S(1)}, f32[184,256]{1,0:T(8,128)S(1)}, u32[]{:S(2)}, u32[]{:S(2)}) collective-permute-start(f32[184,256]{1,0:T(8,128)S(1)} %add.291), channel_id=1, source_target_pairs={{0,128},{64,192},{128,0},{192,64},{256,384},{320,448},{384,256},{4... | collective-permute-start | bytes 565256 | tf_op jit(solution)/shard_map/ppermute | solution.py:261
  126.9 11.6 %collective-permute-start.12 = (f32[184,256]{1,0:T(8,128)S(1)}, f32[184,256]{1,0:T(8,128)S(1)}, u32[]{:S(2)}, u32[]{:S(2)}) collective-permute-start(f32[184,256]{1,0:T(8,128)S(1)} %add.292), channel_id=1, source_target_pairs={{0,256},{64,320},{128,384},{192,448},{256,0},{320,64},{384,128},{4... | collective-permute-start | bytes 565256 | tf_op jit(solution)/shard_map/ppermute | solution.py:261
  138.5 8.4 %collective-permute-start.13 = (bf16[184,256]{1,0:T(8,128)(2,1)S(1)}, bf16[184,256]{1,0:T(8,128)(2,1)S(1)}, u32[]{:S(2)}, u32[]{:S(2)}) collective-permute-start(bf16[184,256]{1,0:T(8,128)(2,1)S(1)} %add_convert_fusion.2), channel_id=1, source_target_pairs={{0,32},{16,48},{32,0},{48,16},{1,33},{17,49},{33,1},{49,17},{2,34}... | collective-permute-start | bytes 282632 | tf_op jit(solution)/shard_map/ppermute | solution.py:271
  146.9 6.3 %collective-permute-start.14 = (bf16[368,256]{1,0:T(8,128)(2,1)S(1)}, bf16[368,256]{1,0:T(8,128)(2,1)S(1)}, u32[]{:S(2)}, u32[]{:S(2)}) collective-permute-start(bf16[368,256]{1,0:T(8,128)(2,1)S(1)} %constant_dynamic-update-slice_fusion.3), channel_id=1, source_target_pairs={{0,16},{16,0},{32,48},{48,32},{1,17},{17,1},{33,49},{49,33},{2,18}... | collective-permute-start | bytes 565256 | tf_op jit(solution)/shard_map/ppermute | solution.py:271
  153.2 15.6 %collective-permute-start.15 = (bf16[736,256]{1,0:T(8,128)(2,1)S(1)}, bf16[736,256]{1,0:T(8,128)(2,1)S(1)}, u32[]{:S(2)}, u32[]{:S(2)}) collective-permute-start(bf16[736,256]{1,0:T(8,128)(2,1)S(1)} %constant_dynamic-update-slice_fusion.2), channel_id=1, source_target_pairs={{0,2},{1,3},{2,0},{3,1},{4,6},{5,7},{6,4},{7,5},{8,10},{9,11},{10,... | collective-permute-start | bytes 1130504 | tf_op jit(solution)/shard_map/ppermute | solution.py:271
  168.9 20.0 %collective-permute-start.16 = (bf16[1472,256]{1,0:T(8,128)(2,1)S(1)}, bf16[1472,256]{1,0:T(8,128)(2,1)S(1)}, u32[]{:S(2)}, u32[]{:S(2)}) collective-permute-start(bf16[1472,256]{1,0:T(8,128)(2,1)S(1)} %constant_dynamic-update-slice_fusion.1), channel_id=1, source_target_pairs={{0,1},{1,0},{2,3},{3,2},{4,5},{5,4},{6,7},{7,6},{8,9},{9,8},{10,11... | collective-permute-start | bytes 2261000 | tf_op jit(solution)/shard_map/ppermute | solution.py:271
where the time goes:
time: 193 us; the launch traced here: 192 us
  starting transfers between devices  70.6 us (37%)
  waiting for transfers between devices  61 us (32%)
  blocking collectives  18 us (9%)
  other arithmetic  15 us (8%)
  local copies, waits for them, and re-layouts  13 us (7%)
  matrix products  12.9 us (7%)
    ppermute x4, starting transfers between devices, butterfly_gather(): got = lax.ppermute(flat, axis, [(j, j ^ step) for j in range(count)])  38.6 us
    ppermute x3, waiting for transfers between devices, per_device(): upstream = lax.ppermute(carried, 'section', [(active + 1, active)])  19.1 us
    ppermute x3, waiting for transfers between devices, butterfly_sum(): lax.ppermute(flat, axis, [(j, j ^ step) for j in range(count)])  19 us
    ppermute x4, waiting for transfers between devices, butterfly_gather(): got = lax.ppermute(flat, axis, [(j, j ^ step) for j in range(count)])  11.4 us
    all_gather x1, blocking collectives, per_device(): out_grad = lax.all_gather(out_grad, 'space', axis=1, tiled=True)  10.5 us
    ppermute x2, waiting for transfers between devices, butterfly_scatter(): lax.ppermute(sent, axis, [(j, j ^ step) for j in range(count)])  9.03 us
    ppermute x3, starting transfers between devices, butterfly_sum(): lax.ppermute(flat, axis, [(j, j ^ step) for j in range(count)])  8.07 us
    ppermute x2, starting transfers between devices, butterfly_scatter(): lax.ppermute(sent, axis, [(j, j ^ step) for j in range(count)])  7.79 us
  transfers between devices with their start and end apart: 17, of which 11 were waited for; matrix products, arithmetic and copies ran while one was open for 11% of the time, Pallas kernels for 0%

commit v1 on v0

--- a/solution.py
+++ b/solution.py
@@ -173,7 +173,15 @@
     section_count = lax.axis_size("section")
     section_no = lax.axis_index("section")
     images = lax.all_gather(images, "space", axis=1, tiled=True)
-    out_grad = lax.all_gather(out_grad, "space", axis=1, tiled=True)
+    out_grad = jnp.concatenate(
+        lax.all_to_all(
+            jnp.stack([out_grad] * lax.axis_size("space"), axis=0),
+            axis_name="space",
+            split_axis=0,
+            concat_axis=0,
+        ),
+        axis=1,
+    )
     row_count = images.shape[1]
     col_count = images.shape[2]
     channels = images.shape[3]

time: 193 us -> 190 us (0.984)
  the two profiles are of different devices: /device:TPU:25 before, /device:TPU:7 now
where the time goes in v1:
time: 190 us
  starting transfers between devices  79.1 us (42%)
  waiting for transfers between devices  57.6 us (30%)
  other arithmetic  15 us (8%)
  matrix products  14.8 us (8%)
  local copies, waits for them, and re-layouts  14 us (7%)
  blocking collectives  7.48 us (4%)
    ppermute x4, starting transfers between devices, butterfly_gather(): got = lax.ppermute(flat, axis, [(j, j ^ step) for j in range(count)])  38.7 us
    ppermute x3, waiting for transfers between devices, per_device(): upstream = lax.ppermute(carried, 'section', [(active + 1, active)])  19.1 us
    ppermute x3, starting transfers between devices, butterfly_sum(): lax.ppermute(flat, axis, [(j, j ^ step) for j in range(count)])  14.5 us
    ppermute x4, waiting for transfers between devices, butterfly_gather(): got = lax.ppermute(flat, axis, [(j, j ^ step) for j in range(count)])  12.6 us
    ppermute x3, waiting for transfers between devices, butterfly_sum(): lax.ppermute(flat, axis, [(j, j ^ step) for j in range(count)])  12.1 us
    ppermute x2, waiting for transfers between devices, butterfly_scatter(): lax.ppermute(sent, axis, [(j, j ^ step) for j in range(count)])  10.5 us
    all_gather x1, blocking collectives, per_device(): images = lax.all_gather(images, 'space', axis=1, tiled=True)  7.48 us
    ppermute x3, starting transfers between devices, per_device(): inputs = lax.ppermute(carried, 'section', [(moment - 1, moment)])  7.36 us
  transfers between devices with their start and end apart: 18, of which 11 were waited for; matrix products, arithmetic and copies ran while one was open for 13% of the time, Pallas kernels for 0%

profile of v1, /device:TPU:7, one launch (start us, length us, event | category | flops | bytes accessed | tf_op | source)
XLA Modules:
  0.0 189.8 jit_solution(8575595817062132129)
XLA Ops:
  0.7 7.5 %all_gather.3 = bf16[2,4,64,256]{3,2,0,1:T(8,128)(2,1)S(1)} all-gather(bf16[2,1,64,256]{3,2,0,1:T(8,128)(2,1)} %bitcast.176), channel_id=1, replica_groups=mesh['dy'=8,'dx'=4,'section'=4,'space'=4] {'space'}, dimensions={1}, use_global_device_ids=true | all-gather | bytes 327680 | tf_op jit(solution)/shard_map/all_gather | solution.py:175
  9.2 1.2 fusion.132
  10.6 0.9 broadcast_multiply_fusion.3
  11.5 1.2 fusion.223
  13.6 0.9 convolution_select_fusion.6
  15.1 5.8 %collective-permute-start = (bf16[2,4,64,256]{3,1,2,0:T(4,128)(2,1)S(1)}, bf16[2,4,64,256]{3,1,2,0:T(4,128)(2,1)S(1)}, u32[]{:S(2)}, u32[]{:S(2)}) collective-permute-start(bf16[2,4,64,256]{3,1,2,0:T(4,128)(2,1)S(1)} %fusion.79), channel_id=1, source_target_pairs={{0,4},{1,5},{2,6},{3,7},{16,20},{17,21},{18,22},{19,23},{32,36},{3... | collective-permute-start | bytes 786440 | tf_op jit(solution)/shard_map/ppermute | solution.py:203
  21.0 4.7 %collective-permute-start.3 = (bf16[2,4,64,256]{3,1,2,0:T(4,128)(2,1)S(1)}, bf16[2,4,64,256]{3,1,2,0:T(4,128)(2,1)S(1)}, u32[]{:S(2)}, u32[]{:S(2)}) collective-permute-start(bf16[2,4,64,256]{3,1,2,0:T(4,128)(2,1)S(1)} %fusion.79), channel_id=1, source_target_pairs={{0,12},{1,13},{2,14},{3,15},{16,28},{17,29},{18,30},{19,31},{32,44... | collective-permute-start | bytes 786440 | tf_op jit(solution)/shard_map/ppermute | solution.py:208
  25.7 0.7 stack.2
  26.4 3.8 %all-to-all-start = ((bf16[4,2,1,64,256]{4,3,1,2,0:T(8,128)(2,1)}), bf16[4,2,1,64,256]{4,3,1,2,0:T(8,128)(2,1)S(1)}, u32[]{:S(2)}, u32[]{:S(2)}) async-start(bf16[4,2,1,64,256]{4,3,1,2,0:T(8,128)(2,1)} %stack.2), calls=%async_computation | async-start | bytes 524288 | tf_op jit(solution)/shard_map/all_to_all | solution.py:177
  31.2 0.9 broadcast_multiply_fusion.2
  33.4 0.9 convolution_select_fusion.5
  34.8 0.9 collective-permute-start.1
  37.3 1.6 convolution_select_fusion.3
  41.3 0.9 convolution_select_fusion.4
  42.8 0.7 collective-permute-start.2
  44.8 1.8 multiply_reduce_fusion
  48.2 1.5 collective-permute-start.7
  52.1 0.9 convolution_select_fusion.2
  53.4 0.7 multiply_reduce_fusion.1
  55.0 0.7 collective-permute-start.5
  56.9 0.9 convolution_select_fusion.1
  58.2 0.7 multiply_reduce_fusion.2
  59.9 1.6 collective-permute-start.6
  61.8 1.6 copy.80
  63.4 3.3 %collective-permute-done.7 = bf16[2,4,64,256]{3,1,2,0:T(4,128)(2,1)S(1)} collective-permute-done((bf16[2,4,64,256]{3,1,2,0:T(4,128)(2,1)S(1)}, bf16[2,4,64,256]{3,1,2,0:T(4,128)(2,1)S(1)}, u32[]{:S(2)}, u32[]{:S(2)}) %collective-permute-start.7) | collective-permute-done | bytes 262176 | tf_op jit(solution)/shard_map/ppermute | solution.py:228
  66.7 19.1 %collective-permute-done.6 = bf16[2,4,64,256]{3,1,2,0:T(4,128)(2,1)S(1)} collective-permute-done((bf16[2,4,64,256]{3,1,2,0:T(4,128)(2,1)S(1)}, bf16[2,4,64,256]{3,1,2,0:T(4,128)(2,1)S(1)}, u32[]{:S(2)}, u32[]{:S(2)}) %collective-permute-start.6) | collective-permute-done | bytes 262176 | tf_op jit(solution)/shard_map/ppermute | solution.py:219
  87.4 0.9 convolution_select_fusion
  89.6 1.8 fusion.55
  91.6 2.5 %collective-permute-start.8 = (f32[368,256]{1,0:T(8,128)S(1)}, f32[368,256]{1,0:T(8,128)S(1)}, u32[]{:S(2)}, u32[]{:S(2)}) collective-permute-start(f32[368,256]{1,0:T(8,128)S(1)} %constant_dynamic-slice_fusion.2), channel_id=1, source_target_pairs={{0,16},{16,0},{32,48},{48,32},{1,17},{17,1},{33,49},{49,33},{2,18}... | collective-permute-start | bytes 1130504 | tf_op jit(solution)/shard_map/ppermute | solution.py:260
  94.2 5.8 %collective-permute-done.8 = f32[368,256]{1,0:T(8,128)S(1)} collective-permute-done((f32[368,256]{1,0:T(8,128)S(1)}, f32[368,256]{1,0:T(8,128)S(1)}, u32[]{:S(2)}, u32[]{:S(2)}) %collective-permute-start.8) | collective-permute-done | bytes 376864 | tf_op jit(solution)/shard_map/ppermute | solution.py:260
  100.1 3.1 %collective-permute-start.9 = (f32[184,256]{1,0:T(8,128)S(1)}, f32[184,256]{1,0:T(8,128)S(1)}, u32[]{:S(2)}, u32[]{:S(2)}) collective-permute-start(f32[184,256]{1,0:T(8,128)S(1)} %constant_dynamic-slice_fusion.1), channel_id=1, source_target_pairs={{0,32},{16,48},{32,0},{48,16},{1,33},{17,49},{33,1},{49,17},{2,34}... | collective-permute-start | bytes 565256 | tf_op jit(solution)/shard_map/ppermute | solution.py:260
  103.2 4.7 %collective-permute-done.9 = f32[184,256]{1,0:T(8,128)S(1)} collective-permute-done((f32[184,256]{1,0:T(8,128)S(1)}, f32[184,256]{1,0:T(8,128)S(1)}, u32[]{:S(2)}, u32[]{:S(2)}) %collective-permute-start.9) | collective-permute-done | bytes 188448 | tf_op jit(solution)/shard_map/ppermute | solution.py:260
  107.9 3.3 %collective-permute-start.10 = (f32[184,256]{1,0:T(8,128)S(1)}, f32[184,256]{1,0:T(8,128)S(1)}, u32[]{:S(2)}, u32[]{:S(2)}) collective-permute-start(f32[184,256]{1,0:T(8,128)S(1)} %dynamic-slice_add_fusion.1), channel_id=1, source_target_pairs={{0,64},{64,0},{128,192},{192,128},{256,320},{320,256},{384,448},{4... | collective-permute-start | bytes 565256 | tf_op jit(solution)/shard_map/ppermute | solution.py:269
  111.2 3.3 %collective-permute-done.10 = f32[184,256]{1,0:T(8,128)S(1)} collective-permute-done((f32[184,256]{1,0:T(8,128)S(1)}, f32[184,256]{1,0:T(8,128)S(1)}, u32[]{:S(2)}, u32[]{:S(2)}) %collective-permute-start.10) | collective-permute-done | bytes 188448 | tf_op jit(solution)/shard_map/ppermute | solution.py:269
  114.6 4.1 %collective-permute-start.11 = (f32[184,256]{1,0:T(8,128)S(1)}, f32[184,256]{1,0:T(8,128)S(1)}, u32[]{:S(2)}, u32[]{:S(2)}) collective-permute-start(f32[184,256]{1,0:T(8,128)S(1)} %add.291), channel_id=1, source_target_pairs={{0,128},{64,192},{128,0},{192,64},{256,384},{320,448},{384,256},{4... | collective-permute-start | bytes 565256 | tf_op jit(solution)/shard_map/ppermute | solution.py:269
  118.7 5.0 %collective-permute-done.11 = f32[184,256]{1,0:T(8,128)S(1)} collective-permute-done((f32[184,256]{1,0:T(8,128)S(1)}, f32[184,256]{1,0:T(8,128)S(1)}, u32[]{:S(2)}, u32[]{:S(2)}) %collective-permute-start.11) | collective-permute-done | bytes 188448 | tf_op jit(solution)/shard_map/ppermute | solution.py:269
  123.8 7.0 %collective-permute-start.12 = (f32[184,256]{1,0:T(8,128)S(1)}, f32[184,256]{1,0:T(8,128)S(1)}, u32[]{:S(2)}, u32[]{:S(2)}) collective-permute-start(f32[184,256]{1,0:T(8,128)S(1)} %add.292), channel_id=1, source_target_pairs={{0,256},{64,320},{128,384},{192,448},{256,0},{320,64},{384,128},{4... | collective-permute-start | bytes 565256 | tf_op jit(solution)/shard_map/ppermute | solution.py:269
  130.8 3.7 %collective-permute-done.12 = f32[184,256]{1,0:T(8,128)S(1)} collective-permute-done((f32[184,256]{1,0:T(8,128)S(1)}, f32[184,256]{1,0:T(8,128)S(1)}, u32[]{:S(2)}, u32[]{:S(2)}) %collective-permute-start.12) | collective-permute-done | bytes 188448 | tf_op jit(solution)/shard_map/ppermute | solution.py:269
  134.6 5.7 %collective-permute-start.13 = (bf16[184,256]{1,0:T(8,128)(2,1)S(1)}, bf16[184,256]{1,0:T(8,128)(2,1)S(1)}, u32[]{:S(2)}, u32[]{:S(2)}) collective-permute-start(bf16[184,256]{1,0:T(8,128)(2,1)S(1)} %add_convert_fusion.2), channel_id=1, source_target_pairs={{0,32},{16,48},{32,0},{48,16},{1,33},{17,49},{33,1},{49,17},{2,34}... | collective-permute-start | bytes 282632 | tf_op jit(solution)/shard_map/ppermute | solution.py:279
  140.3 1.9 %collective-permute-done.13 = bf16[184,256]{1,0:T(8,128)(2,1)S(1)} collective-permute-done((bf16[184,256]{1,0:T(8,128)(2,1)S(1)}, bf16[184,256]{1,0:T(8,128)(2,1)S(1)}, u32[]{:S(2)}, u32[]{:S(2)}) %collective-permute-start.13) | collective-permute-done | bytes 94240 | tf_op jit(solution)/shard_map/ppermute | solution.py:279
  142.2 2.4 %collective-permute-start.14 = (bf16[368,256]{1,0:T(8,128)(2,1)S(1)}, bf16[368,256]{1,0:T(8,128)(2,1)S(1)}, u32[]{:S(2)}, u32[]{:S(2)}) collective-permute-start(bf16[368,256]{1,0:T(8,128)(2,1)S(1)} %constant_dynamic-update-slice_fusion.3), channel_id=1, source_target_pairs={{0,16},{16,0},{32,48},{48,32},{1,17},{17,1},{33,49},{49,33},{2,18}... | collective-permute-start | bytes 565256 | tf_op jit(solution)/shard_map/ppermute | solution.py:279
  144.7 4.1 %collective-permute-done.14 = bf16[368,256]{1,0:T(8,128)(2,1)S(1)} collective-permute-done((bf16[368,256]{1,0:T(8,128)(2,1)S(1)}, bf16[368,256]{1,0:T(8,128)(2,1)S(1)}, u32[]{:S(2)}, u32[]{:S(2)}) %collective-permute-start.14) | collective-permute-done | bytes 188448 | tf_op jit(solution)/shard_map/ppermute | solution.py:279
  148.9 9.6 %collective-permute-start.15 = (bf16[736,256]{1,0:T(8,128)(2,1)S(1)}, bf16[736,256]{1,0:T(8,128)(2,1)S(1)}, u32[]{:S(2)}, u32[]{:S(2)}) collective-permute-start(bf16[736,256]{1,0:T(8,128)(2,1)S(1)} %constant_dynamic-update-slice_fusion.2), channel_id=1, source_target_pairs={{0,2},{1,3},{2,0},{3,1},{4,6},{5,7},{6,4},{7,5},{8,10},{9,11},{10,... | collective-permute-start | bytes 1130504 | tf_op jit(solution)/shard_map/ppermute | solution.py:279
  158.6 4.9 %collective-permute-done.15 = bf16[736,256]{1,0:T(8,128)(2,1)S(1)} collective-permute-done((bf16[736,256]{1,0:T(8,128)(2,1)S(1)}, bf16[736,256]{1,0:T(8,128)(2,1)S(1)}, u32[]{:S(2)}, u32[]{:S(2)}) %collective-permute-start.15) | collective-permute-done | bytes 376864 | tf_op jit(solution)/shard_map/ppermute | solution.py:279
  163.5 21.0 %collective-permute-start.16 = (bf16[1472,256]{1,0:T(8,128)(2,1)S(1)}, bf16[1472,256]{1,0:T(8,128)(2,1)S(1)}, u32[]{:S(2)}, u32[]{:S(2)}) collective-permute-start(bf16[1472,256]{1,0:T(8,128)(2,1)S(1)} %constant_dynamic-update-slice_fusion.1), channel_id=1, source_target_pairs={{0,1},{1,0},{2,3},{3,2},{4,5},{5,4},{6,7},{7,6},{8,9},{9,8},{10,11... | collective-permute-start | bytes 2261000 | tf_op jit(solution)/shard_map/ppermute | solution.py:279
  184.7 1.7 collective-permute-done.16
  186.7 1.6 slice.95
  188.9 0.9 reshape.176
  (150 shorter events, 23.6 us)
Async XLA Ops:
  0.6 12.9 %copy-start = (bf16[1,3,3,256,256]{4,3,2,1,0:T(8,128)(2,1)S(1)}, bf16[1,3,3,256,256]{4,3,2,1,0:T(8,128)(2,1)}, u32[]{:S(2)}) copy-start(bf16[1,3,3,256,256]{4,3,2,1,0:T(8,128)(2,1)} %param.9) | copy-start | bytes 3538948
  0.6 12.9 %copy-start.9 = (pred[16,9]{0,1:T(8,128)(4,1)S(1)}, pred[16,9]{0,1:T(8,128)(4,1)}, u32[]{:S(2)}) copy-start(pred[16,9]{0,1:T(8,128)(4,1)} %constant.217) | copy-start | bytes 436
  0.7 30.6 %copy-start.7 = (s32[256]{0:T(256)}, s32[256]{0:T(256)S(1)}, u32[]{:S(2)}) copy-start(s32[256]{0:T(256)S(1)} %and_select_fusion) | copy-start | bytes 3076
  9.2 4.0 %copy-start.3 = (f32[2,128]{1,0:T(2,128)}, f32[2,128]{1,0:T(2,128)S(1)}, u32[]{:S(2)}) copy-start(f32[2,128]{1,0:T(2,128)S(1)} %get-tuple-element.49) | copy-start | bytes 3076
  9.2 4.0 %copy-start.5 = (f32[2,128]{1,0:T(2,128)}, f32[2,128]{1,0:T(2,128)S(1)}, u32[]{:S(2)}) copy-start(f32[2,128]{1,0:T(2,128)S(1)} %get-tuple-element.50) | copy-start | bytes 3076
  10.6 3.8 %copy-start.11 = (f32[2,256]{1,0:T(2,128)}, f32[2,256]{1,0:T(2,128)S(1)}, u32[]{:S(2)}) copy-start(f32[2,256]{1,0:T(2,128)S(1)} %fusion.31) | copy-start | bytes 6148
  13.6 12.1 %copy-start.2 = (bf16[2,1,64,256]{3,2,1,0:T(8,128)(2,1)S(1)}, bf16[2,1,64,256]{3,2,1,0:T(8,128)(2,1)}, u32[]{:S(2)}) copy-start(bf16[2,1,64,256]{3,2,1,0:T(8,128)(2,1)} %param.8) | copy-start | bytes 196612
  14.5 15.8 %copy-start.1 = (f32[1,256]{1,0:T(1,128)S(1)}, f32[1,256]{1,0:T(1,128)}, u32[]{:S(2)}) copy-start(f32[1,256]{1,0:T(1,128)} %param.10) | copy-start | bytes 3076
  15.1 15.6 %collective-permute-start = (bf16[2,4,64,256]{3,1,2,0:T(4,128)(2,1)S(1)}, bf16[2,4,64,256]{3,1,2,0:T(4,128)(2,1)S(1)}, u32[]{:S(2)}, u32[]{:S(2)}) collective-permute-start(bf16[2,4,64,256]{3,1,2,0:T(4,128)(2,1)S(1)} %fusion.79), channel_id=1, source_target_pairs={{0,4},{1,5},{2,6},{3,7},{16,20},{17,21},{18,22},{19,23},{32,36},{3... | collective-permute-start | bytes 786440 | tf_op jit(solution)/shard_map/ppermute | solution.py:203
  21.0 22.9 %collective-permute-start.3 = (bf16[2,4,64,256]{3,1,2,0:T(4,128)(2,1)S(1)}, bf16[2,4,64,256]{3,1,2,0:T(4,128)(2,1)S(1)}, u32[]{:S(2)}, u32[]{:S(2)}) collective-permute-start(bf16[2,4,64,256]{3,1,2,0:T(4,128)(2,1)S(1)} %fusion.79), channel_id=1, source_target_pairs={{0,12},{1,13},{2,14},{3,15},{16,28},{17,29},{18,30},{19,31},{32,44... | collective-permute-start | bytes 786440 | tf_op jit(solution)/shard_map/ppermute | solution.py:208
  26.4 9.7 %all-to-all-start = ((bf16[4,2,1,64,256]{4,3,1,2,0:T(8,128)(2,1)}), bf16[4,2,1,64,256]{4,3,1,2,0:T(8,128)(2,1)S(1)}, u32[]{:S(2)}, u32[]{:S(2)}) async-start(bf16[4,2,1,64,256]{4,3,1,2,0:T(8,128)(2,1)} %stack.2), calls=%async_computation | async-start | bytes 524288 | tf_op jit(solution)/shard_map/all_to_all | solution.py:177
  31.2 3.1 %copy-start.13 = (f32[2,256]{1,0:T(2,128)}, f32[2,256]{1,0:T(2,128)S(1)}, u32[]{:S(2)}) copy-start(f32[2,256]{1,0:T(2,128)S(1)} %fusion.27) | copy-start | bytes 6148
  34.8 4.4 %collective-permute-start.1 = (bf16[2,4,64,256]{3,1,2,0:T(4,128)(2,1)S(1)}, bf16[2,4,64,256]{3,1,2,0:T(4,128)(2,1)S(1)}, u32[]{:S(2)}, u32[]{:S(2)}) collective-permute-start(bf16[2,4,64,256]{3,1,2,0:T(4,128)(2,1)S(1)} %fusion.85), channel_id=1, source_target_pairs={{4,8},{5,9},{6,10},{7,11},{20,24},{21,25},{22,26},{23,27},{36,40},... | collective-permute-start | bytes 786440 | tf_op jit(solution)/shard_map/ppermute | solution.py:203
  37.2 2.2 %copy-start.8 = (s32[256]{0:T(256)S(1)}, s32[256]{0:T(256)}, u32[]{:S(2)}) copy-start(s32[256]{0:T(256)} %copy-done.7) | copy-start | bytes 3076
  38.8 2.5 %copy-start.10 = (pred[16,9]{0,1:T(8,128)(4,1)S(1)}, pred[16,9]{0,1:T(8,128)(4,1)}, u32[]{:S(2)}) copy-start(pred[16,9]{0,1:T(8,128)(4,1)} %constant.217) | copy-start | bytes 436
  42.2 2.3 %copy-start.12 = (f32[2,256]{1,0:T(2,128)S(1)}, f32[2,256]{1,0:T(2,128)}, u32[]{:S(2)}) copy-start(f32[2,256]{1,0:T(2,128)} %copy-done.11) | copy-start | bytes 6148
  42.2 2.3 %copy-start.14 = (f32[2,256]{1,0:T(2,128)S(1)}, f32[2,256]{1,0:T(2,128)}, u32[]{:S(2)}) copy-start(f32[2,256]{1,0:T(2,128)} %copy-done.13) | copy-start | bytes 6148
  42.2 2.3 %copy-start.15 = (f32[2,256]{1,0:T(2,128)S(1)}, f32[2,256]{1,0:T(2,128)}, u32[]{:S(2)}) copy-start(f32[2,256]{1,0:T(2,128)} %get-tuple-element.51) | copy-start | bytes 6148
  42.2 2.3 %copy-start.16 = (f32[2,256]{1,0:T(2,128)S(1)}, f32[2,256]{1,0:T(2,128)}, u32[]{:S(2)}) copy-start(f32[2,256]{1,0:T(2,128)} %get-tuple-element.52) | copy-start | bytes 6148
  42.8 1.1 collective-permute-start.2
  47.5 3.7 %collective-permute-start.4 = (bf16[2,4,64,256]{3,1,2,0:T(4,128)(2,1)S(1)}, bf16[2,4,64,256]{3,1,2,0:T(4,128)(2,1)S(1)}, u32[]{:S(2)}, u32[]{:S(2)}) collective-permute-start(bf16[2,4,64,256]{3,1,2,0:T(4,128)(2,1)S(1)} %fusion.94), channel_id=1, source_target_pairs={{12,8},{13,9},{14,10},{15,11},{28,24},{29,25},{30,26},{31,27},{44,... | collective-permute-start | bytes 786440 | tf_op jit(solution)/shard_map/ppermute | solution.py:219
  48.2 18.5 %collective-permute-start.7 = (bf16[2,4,64,256]{3,1,2,0:T(4,128)(2,1)S(1)}, bf16[2,4,64,256]{3,1,2,0:T(4,128)(2,1)S(1)}, u32[]{:S(2)}, u32[]{:S(2)}) collective-permute-start(bf16[2,4,64,256]{3,1,2,0:T(4,128)(2,1)S(1)} %fusion.94), channel_id=1, source_target_pairs={{12,0},{13,1},{14,2},{15,3},{28,16},{29,17},{30,18},{31,19},{44,32... | collective-permute-start | bytes 786440 | tf_op jit(solution)/shard_map/ppermute | solution.py:228
  55.0 1.1 collective-permute-start.5
  59.9 26.0 %collective-permute-start.6 = (bf16[2,4,64,256]{3,1,2,0:T(4,128)(2,1)S(1)}, bf16[2,4,64,256]{3,1,2,0:T(4,128)(2,1)S(1)}, u32[]{:S(2)}, u32[]{:S(2)}) collective-permute-start(bf16[2,4,64,256]{3,1,2,0:T(4,128)(2,1)S(1)} %fusion.100), channel_id=1, source_target_pairs={{4,0},{5,1},{6,2},{7,3},{20,16},{21,17},{22,18},{23,19},{36,32},{3... | collective-permute-start | bytes 786440 | tf_op jit(solution)/shard_map/ppermute | solution.py:219
  87.3 1.8 copy-start.4
  87.3 1.8 copy-start.6
  91.6 8.3 %collective-permute-start.8 = (f32[368,256]{1,0:T(8,128)S(1)}, f32[368,256]{1,0:T(8,128)S(1)}, u32[]{:S(2)}, u32[]{:S(2)}) collective-permute-start(f32[368,256]{1,0:T(8,128)S(1)} %constant_dynamic-slice_fusion.2), channel_id=1, source_target_pairs={{0,16},{16,0},{32,48},{48,32},{1,17},{17,1},{33,49},{49,33},{2,18}... | collective-permute-start | bytes 1130504 | tf_op jit(solution)/shard_map/ppermute | solution.py:260
  100.1 7.8 %collective-permute-start.9 = (f32[184,256]{1,0:T(8,128)S(1)}, f32[184,256]{1,0:T(8,128)S(1)}, u32[]{:S(2)}, u32[]{:S(2)}) collective-permute-start(f32[184,256]{1,0:T(8,128)S(1)} %constant_dynamic-slice_fusion.1), channel_id=1, source_target_pairs={{0,32},{16,48},{32,0},{48,16},{1,33},{17,49},{33,1},{49,17},{2,34}... | collective-permute-start | bytes 565256 | tf_op jit(solution)/shard_map/ppermute | solution.py:260
  107.9 6.6 %collective-permute-start.10 = (f32[184,256]{1,0:T(8,128)S(1)}, f32[184,256]{1,0:T(8,128)S(1)}, u32[]{:S(2)}, u32[]{:S(2)}) collective-permute-start(f32[184,256]{1,0:T(8,128)S(1)} %dynamic-slice_add_fusion.1), channel_id=1, source_target_pairs={{0,64},{64,0},{128,192},{192,128},{256,320},{320,256},{384,448},{4... | collective-permute-start | bytes 565256 | tf_op jit(solution)/shard_map/ppermute | solution.py:269
  114.6 9.2 %collective-permute-start.11 = (f32[184,256]{1,0:T(8,128)S(1)}, f32[184,256]{1,0:T(8,128)S(1)}, u32[]{:S(2)}, u32[]{:S(2)}) collective-permute-start(f32[184,256]{1,0:T(8,128)S(1)} %add.291), channel_id=1, source_target_pairs={{0,128},{64,192},{128,0},{192,64},{256,384},{320,448},{384,256},{4... | collective-permute-start | bytes 565256 | tf_op jit(solution)/shard_map/ppermute | solution.py:269
  123.8 10.8 %collective-permute-start.12 = (f32[184,256]{1,0:T(8,128)S(1)}, f32[184,256]{1,0:T(8,128)S(1)}, u32[]{:S(2)}, u32[]{:S(2)}) collective-permute-start(f32[184,256]{1,0:T(8,128)S(1)} %add.292), channel_id=1, source_target_pairs={{0,256},{64,320},{128,384},{192,448},{256,0},{320,64},{384,128},{4... | collective-permute-start | bytes 565256 | tf_op jit(solution)/shard_map/ppermute | solution.py:269
  134.6 7.6 %collective-permute-start.13 = (bf16[184,256]{1,0:T(8,128)(2,1)S(1)}, bf16[184,256]{1,0:T(8,128)(2,1)S(1)}, u32[]{:S(2)}, u32[]{:S(2)}) collective-permute-start(bf16[184,256]{1,0:T(8,128)(2,1)S(1)} %add_convert_fusion.2), channel_id=1, source_target_pairs={{0,32},{16,48},{32,0},{48,16},{1,33},{17,49},{33,1},{49,17},{2,34}... | collective-permute-start | bytes 282632 | tf_op jit(solution)/shard_map/ppermute | solution.py:279
  142.2 6.6 %collective-permute-start.14 = (bf16[368,256]{1,0:T(8,128)(2,1)S(1)}, bf16[368,256]{1,0:T(8,128)(2,1)S(1)}, u32[]{:S(2)}, u32[]{:S(2)}) collective-permute-start(bf16[368,256]{1,0:T(8,128)(2,1)S(1)} %constant_dynamic-update-slice_fusion.3), channel_id=1, source_target_pairs={{0,16},{16,0},{32,48},{48,32},{1,17},{17,1},{33,49},{49,33},{2,18}... | collective-permute-start | bytes 565256 | tf_op jit(solution)/shard_map/ppermute | solution.py:279
  148.9 14.6 %collective-permute-start.15 = (bf16[736,256]{1,0:T(8,128)(2,1)S(1)}, bf16[736,256]{1,0:T(8,128)(2,1)S(1)}, u32[]{:S(2)}, u32[]{:S(2)}) collective-permute-start(bf16[736,256]{1,0:T(8,128)(2,1)S(1)} %constant_dynamic-update-slice_fusion.2), channel_id=1, source_target_pairs={{0,2},{1,3},{2,0},{3,1},{4,6},{5,7},{6,4},{7,5},{8,10},{9,11},{10,... | collective-permute-start | bytes 1130504 | tf_op jit(solution)/shard_map/ppermute | solution.py:279
  163.5 22.8 %collective-permute-start.16 = (bf16[1472,256]{1,0:T(8,128)(2,1)S(1)}, bf16[1472,256]{1,0:T(8,128)(2,1)S(1)}, u32[]{:S(2)}, u32[]{:S(2)}) collective-permute-start(bf16[1472,256]{1,0:T(8,128)(2,1)S(1)} %constant_dynamic-update-slice_fusion.1), channel_id=1, source_target_pairs={{0,1},{1,0},{2,3},{3,2},{4,5},{5,4},{6,7},{7,6},{8,9},{9,8},{10,11... | collective-permute-start | bytes 2261000 | tf_op jit(solution)/shard_map/ppermute | solution.py:279
